TPU v7x, 32 devices: a whole 2x2x4 slice. The times are simulated.
32 devices in a mesh: group: 8 (over z, x), blk: 4 (over y, core).
Axes of the slice: x: 2, y: 2, z: 4, core: 2. Of those that a mesh axis runs over, the one named last changes fastest.
Arguments:
- sources: bfloat16 [32768, 512], P(('group', 'blk')), may hold values from -20 to 20
- targets: bfloat16 [256, 512], P(('group', 'blk')), may hold values from -20 to 20
- target_potential: bfloat16 [256], P(('group', 'blk')), may hold values from -1.5 to 1.5
- log_source_mass: float32 [32768], P(('group', 'blk')), may hold values from -3 to 0
- log_target_mass: float32 [256], P(('group', 'blk')), may hold values from -3 to 0
Outputs:
- source_potential: float32 [32768], P(('group', 'blk'))
- target_update: float32 [256], P(('group', 'blk'))
All inputs are finite; a program needn't handle non-finite values.
Results may differ from a plain program's by a relative error of at most 0.0003.
Values may be sent and summed in bfloat16 or wider, within the bound.
No kernel may reach another device: no remote copies, remote signals or barrier semaphores. Data moves between devices by JAX's collectives and lax.ppermute only.
A program may use at most 64 MiB of HBM per device.

v0:
```python
import jax
import jax.numpy as jnp
from jax import lax
from jax.sharding import PartitionSpec as P

epsilon = 0.05


def passed_along(block, axis, distance):
    devices = range(lax.axis_size(axis))
    route = [((i - distance) % len(devices), i) for i in devices]
    return lax.ppermute(block, axis, route)


def merged(x, axis, combine):
    everything = jax.tree.map(lambda part: lax.all_gather(part, axis), x)
    first = jax.tree.map(lambda part: part[0], everything)

    def hop(k, so_far):
        return combine(so_far, jax.tree.map(lambda part: part[k], everything))

    return lax.fori_loop(1, lax.axis_size(axis), hop, first)


def scores(source_rows, target_rows, target_pots):
    features = source_rows.shape[1]
    offset = target_pots.astype(jnp.float32) / epsilon - jnp.sum(
        jnp.square(target_rows.astype(jnp.float32)), 1
    ) / (features * epsilon)
    products = lax.dot_general(
        source_rows, target_rows, (((1,), (1,)), ((), ())), preferred_element_type=jnp.float32
    )
    return products * (2.0 / (features * epsilon)) + offset[None, :]


def split_blocks(target_rows, target_pots):
    row_count = target_rows.shape[0]
    block_width = 512 if row_count % 512 == 0 else row_count
    return (
        target_rows.reshape(row_count // block_width, block_width, target_rows.shape[1]),
        target_pots.reshape(row_count // block_width, block_width),
    )


def row_fold(running, source_rows, target_rows, target_pots):

    def advance(state, pieces):
        logits = scores(source_rows, pieces[0], pieces[1])
        run_max, run_sum = state
        new_max = jnp.maximum(run_max, jnp.max(logits, 1))
        new_sum = run_sum * jnp.exp(run_max - new_max) + jnp.sum(
            jnp.exp(logits - new_max[:, None]), 1
        )
        return ((new_max, new_sum), None)

    return lax.scan(advance, running, split_blocks(target_rows, target_pots))[0]


def column_parts(source_rows, source_dual, target_rows, target_pots):

    def single(pieces):
        logits = scores(source_rows, pieces[0], pieces[1])
        logits = logits - pieces[1].astype(jnp.float32)[None, :] / epsilon + source_dual[:, None]
        col_max = jnp.max(logits, 0)
        return (col_max, jnp.sum(jnp.exp(logits - col_max[None, :]), 0))

    col_max, col_sum = lax.map(single, split_blocks(target_rows, target_pots))
    return (col_max.reshape(-1), col_sum.reshape(-1))


def combine(first, second):
    new_max = jnp.maximum(first[0], second[0])
    return (
        new_max,
        first[1] * jnp.exp(first[0] - new_max) + second[1] * jnp.exp(second[0] - new_max),
    )


def per_device(sources, targets, target_potential, log_source_mass, log_target_mass):
    source_count = sources.shape[0]
    target_count = targets.shape[0]
    group_count = lax.axis_size("group")
    cycle_size = lax.axis_size("blk")
    initial = (
        jnp.full((source_count,), -1e30, jnp.float32),
        jnp.zeros((source_count,), jnp.float32),
    )
    gathered = (
        lax.all_gather(targets, "group", axis=0, tiled=True),
        lax.all_gather(target_potential, "group", axis=0, tiled=True),
    )
    own_block = lax.axis_index("blk")
    held = [(own_block, gathered)]
    forward_set = gathered
    backward_set = gathered
    for distance in range(1, cycle_size // 2 + 1):
        forward_set = passed_along((forward_set[0], forward_set[1]), "blk", 1)
        held.append(((own_block - distance) % cycle_size, forward_set))
        if distance <= (cycle_size - 1) // 2:
            backward_set = passed_along((backward_set[0], backward_set[1]), "blk", -1)
            held.append(((own_block + distance) % cycle_size, backward_set))
    running = initial
    for position, pieces in held:
        running = row_fold(running, sources, pieces[0], pieces[1])
    source_dual = log_source_mass - (running[0] + jnp.log(running[1]))
    grid_max = jnp.zeros((group_count, cycle_size, target_count), jnp.float32)
    grid_sum = jnp.zeros((group_count, cycle_size, target_count), jnp.float32)
    for position, pieces in held:
        part_max, part_sum = column_parts(sources, source_dual, pieces[0], pieces[1])
        where_put = (0, position, 0)
        grid_max = lax.dynamic_update_slice(
            grid_max, part_max.reshape(group_count, 1, target_count), where_put
        )
        grid_sum = lax.dynamic_update_slice(
            grid_sum, part_sum.reshape(group_count, 1, target_count), where_put
        )
    col_max = grid_max.reshape(-1)
    col_sum = grid_sum.reshape(-1)
    first_owned = (lax.axis_index("group") * cycle_size + lax.axis_index("blk")) * target_count
    total_max, total_sum = merged((col_max, col_sum), ("group", "blk"), combine)
    owned_max = lax.dynamic_slice_in_dim(total_max, first_owned, target_count)
    owned_sum = lax.dynamic_slice_in_dim(total_sum, first_owned, target_count)
    features = sources.shape[1]
    source_potential = (
        epsilon * source_dual + jnp.sum(jnp.square(sources.astype(jnp.float32)), 1) / features
    )
    target_update = epsilon * (log_target_mass - (owned_max + jnp.log(owned_sum)))
    return (source_potential, target_update)


def solution(mesh):
    return jax.shard_map(
        per_device,
        mesh=mesh,
        in_specs=(
            P(("group", "blk"), None),
            P(("group", "blk"), None),
            P(("group", "blk")),
            P(("group", "blk")),
            P(("group", "blk")),
        ),
        out_specs=(P(("group", "blk")), P(("group", "blk"))),
        check_vma=False,
    )
```

profile of v0, /device:TPU:0, one launch (start us, length us, event | category | flops | bytes accessed | tf_op | source)
XLA Modules:
  0.0 147.5 jit_solution(8099603570743714564)
XLA Ops:
  0.6 0.0 copy-start
  0.6 32.6 %all_gather.12 = bf16[64,512]{1,0:T(8,128)(2,1)S(1)} all-gather(bf16[8,512]{1,0:T(8,128)(2,1)} %param.8), channel_id=1, replica_groups=mesh['group'=8,'blk'=4] {'group'}, dimensions={0}, use_global_device_ids=true | all-gather | bytes 73728 | tf_op jit(solution)/shard_map/all_gather | solution.py:89
  33.3 0.0 collective-permute-start
  33.3 1.7 %collective-permute-start.2 = (bf16[64,512]{1,0:T(8,128)(2,1)S(1)}, bf16[64,512]{1,0:T(8,128)(2,1)S(1)}, u32[]{:S(2)}, u32[]{:S(2)}) collective-permute-start(bf16[64,512]{1,0:T(8,128)(2,1)S(1)} %all_gather.12), channel_id=1, source_target_pairs={{1,0},{2,1},{3,2},{0,3},{5,4},{6,5},{7,6},{4,7},{9,8},{10,9},{11,1... | collective-permute-start | bytes 196616 | tf_op jit(solution)/shard_map/ppermute | solution.py:12
  35.0 1.2 dynamic-slice.8
  36.9 0.9 dynamic-update-slice
  37.8 21.3 %all-reduce = bf16[64]{0:T(256)(128)(2,1)S(1)} all-reduce(bf16[64]{0:T(256)(128)(2,1)S(1)} %dynamic-update-slice), channel_id=1, replica_groups=mesh['group'=8,'blk'=4] {'group'}, use_global_device_ids=true, to_apply=%add | all-reduce | flops 64 | bytes 256
  59.1 0.0 collective-permute-start.1
  59.1 1.7 %collective-permute-start.3 = (bf16[64]{0:T(256)(128)(2,1)S(1)}, bf16[64]{0:T(256)(128)(2,1)S(1)}, u32[]{:S(2)}, u32[]{:S(2)}) collective-permute-start(bf16[64]{0:T(256)(128)(2,1)S(1)} %all-reduce), channel_id=1, source_target_pairs={{1,0},{2,1},{3,2},{0,3},{5,4},{6,5},{7,6},{4,7},{9,8},{10,9},{11,1... | collective-permute-start | bytes 392 | tf_op jit(solution)/shard_map/ppermute | solution.py:12
  60.9 0.1 multiply_reduce_fusion.4
  61.0 1.7 %fusion.14 = (f32[1024]{0:T(1024)S(1)}, f32[1024,64]{0,1:T(8,128)S(1)}) fusion(f32[64]{0:T(128)S(1)} %get-tuple-element.326, bf16[1024,512]{1,0:T(8,128)(2,1)} %param.7, bf16[64,512]{1,0:T(8,128)(2,1)S(1)} %all_gather.12), kind=kOutput, calls=%fused_computation.51 | convolution fusion | flops 67304448 | bytes 1380608 | tf_op jit(solution)/shard_map/while/body/eval_jaxpr/dot_general | solution.py:30
  62.7 0.0 copy-done
  62.7 0.3 multiply_reduce_fusion
  63.0 0.0 collective-permute-done.1
  63.0 0.1 collective-permute-start.5
  63.1 0.0 collective-permute-done
  63.1 1.6 %collective-permute-start.4 = (bf16[64,512]{1,0:T(8,128)(2,1)S(1)}, bf16[64,512]{1,0:T(8,128)(2,1)S(1)}, u32[]{:S(2)}, u32[]{:S(2)}) collective-permute-start(bf16[64,512]{1,0:T(8,128)(2,1)S(1)} %collective-permute-done), channel_id=1, source_target_pairs={{3,0},{0,1},{1,2},{2,3},{7,4},{4,5},{5,6},{6,7},{11,8},{8,9},{9,10... | collective-permute-start | bytes 196616 | tf_op jit(solution)/shard_map/ppermute | solution.py:12
  64.7 0.1 multiply_reduce_fusion.3
  64.8 0.5 fusion.13
  65.3 0.0 collective-permute-done.2
  65.3 0.1 multiply_reduce_fusion.2
  65.4 0.0 collective-permute-done.3
  65.5 0.5 fusion.12
  65.9 0.9 collective-permute-done.4
  66.9 0.1 multiply_reduce_fusion.1
  67.0 0.0 collective-permute-done.5
  67.0 0.0 copy-start.1
  67.0 0.5 fusion.11
  67.5 0.1 exponential_reduce_fusion.4
  67.6 0.1 exponential_reduce_fusion.6
  67.7 0.0 copy-done.1
  67.7 0.6 multiply_add_fusion.1
  68.3 0.2 fusion.7
  68.5 0.0 copy-start.2
  68.5 0.3 exponential_reduce_fusion
  68.9 0.3 exponential_reduce_fusion.1
  69.1 0.1 reshape_reshape.29
  69.2 0.1 reshape_reshape.28
  69.3 0.1 reshape_reshape.30
  69.4 0.1 reshape_reshape.31
  69.5 0.1 dynamic_update_slice.45
  69.7 0.1 reshape.118
  69.7 37.9 %all-gather.1 = f32[32,1,256]{2,1,0:T(1,128)S(1)} all-gather(f32[1,1,256]{2,1,0:T(1,128)S(1)} %reshape.118), channel_id=1, replica_groups=mesh['group'=8,'blk'=4] {'group','blk'}, dimensions={0}, use_global_device_ids=true | all-gather | bytes 33792 | tf_op jit(solution)/shard_map/all_gather | solution.py:16
  107.6 0.1 reshape_reshape.25
  107.7 0.1 reshape_reshape.24
  107.8 0.1 reshape_reshape.26
  107.8 0.1 reshape_reshape.27
  107.9 0.1 dynamic_update_slice.41
  108.1 0.1 reshape.116
  108.2 36.8 %all-gather = f32[32,1,256]{2,1,0:T(1,128)S(1)} all-gather(f32[1,1,256]{2,1,0:T(1,128)S(1)} %reshape.116), channel_id=1, replica_groups=mesh['group'=8,'blk'=4] {'group','blk'}, dimensions={0}, use_global_device_ids=true | all-gather | bytes 33792 | tf_op jit(solution)/shard_map/all_gather | solution.py:16
  145.1 1.8 %while.11 = (s32[]{:T(128)}, f32[256]{0:T(256)S(1)}, f32[256]{0:T(256)S(1)}, f32[32,256]{1,0:T(8,128)S(1)}, f32[32,256]{1,0:T(8,128)S(1)}, /*index=5*/s32[]{:T(128)}, s32[]{:T(128)}, s32[]{:T(128)}) while((s32[]{:T(128)}, f32[256]{0:T(256)S(1)}, f32[256]{0:T(256)S(1)}, f32[32,256]{1,0:T(8,128)S(1)}, f32[32,256]{1,0:T(8,128)S(1)}, ...), condition=%wide.region_22.23_spmd, body=%wide.region_21.22_spmd.sunk | while | flops 1541 | bytes 10371 | solution.py:22
  146.8 0.0 copy-done.2
  146.9 0.6 subtract_multiply_fusion
  (80 shorter events, 1.3 us)
Async XLA Ops:
  0.6 62.0 %copy-start = (bf16[1024,512]{1,0:T(8,128)(2,1)S(1)}, bf16[1024,512]{1,0:T(8,128)(2,1)}, u32[]{:S(2)}) copy-start(bf16[1024,512]{1,0:T(8,128)(2,1)} %param.7) | copy-start | bytes 3145732
  33.3 29.8 %collective-permute-start = (bf16[64,512]{1,0:T(8,128)(2,1)S(1)}, bf16[64,512]{1,0:T(8,128)(2,1)S(1)}, u32[]{:S(2)}, u32[]{:S(2)}) collective-permute-start(bf16[64,512]{1,0:T(8,128)(2,1)S(1)} %all_gather.12), channel_id=1, source_target_pairs={{3,0},{0,1},{1,2},{2,3},{7,4},{4,5},{5,6},{6,7},{11,8},{8,9},{9,10... | collective-permute-start | bytes 196616 | tf_op jit(solution)/shard_map/ppermute | solution.py:12
  33.3 32.0 %collective-permute-start.2 = (bf16[64,512]{1,0:T(8,128)(2,1)S(1)}, bf16[64,512]{1,0:T(8,128)(2,1)S(1)}, u32[]{:S(2)}, u32[]{:S(2)}) collective-permute-start(bf16[64,512]{1,0:T(8,128)(2,1)S(1)} %all_gather.12), channel_id=1, source_target_pairs={{1,0},{2,1},{3,2},{0,3},{5,4},{6,5},{7,6},{4,7},{9,8},{10,9},{11,1... | collective-permute-start | bytes 196616 | tf_op jit(solution)/shard_map/ppermute | solution.py:12
  59.1 3.9 %collective-permute-start.1 = (bf16[64]{0:T(256)(128)(2,1)S(1)}, bf16[64]{0:T(256)(128)(2,1)S(1)}, u32[]{:S(2)}, u32[]{:S(2)}) collective-permute-start(bf16[64]{0:T(256)(128)(2,1)S(1)} %all-reduce), channel_id=1, source_target_pairs={{3,0},{0,1},{1,2},{2,3},{7,4},{4,5},{5,6},{6,7},{11,8},{8,9},{9,10... | collective-permute-start | bytes 392 | tf_op jit(solution)/shard_map/ppermute | solution.py:12
  59.1 6.3 %collective-permute-start.3 = (bf16[64]{0:T(256)(128)(2,1)S(1)}, bf16[64]{0:T(256)(128)(2,1)S(1)}, u32[]{:S(2)}, u32[]{:S(2)}) collective-permute-start(bf16[64]{0:T(256)(128)(2,1)S(1)} %all-reduce), channel_id=1, source_target_pairs={{1,0},{2,1},{3,2},{0,3},{5,4},{6,5},{7,6},{4,7},{9,8},{10,9},{11,1... | collective-permute-start | bytes 392 | tf_op jit(solution)/shard_map/ppermute | solution.py:12
  63.0 3.9 %collective-permute-start.5 = (bf16[64]{0:T(256)(128)(2,1)S(1)}, bf16[64]{0:T(256)(128)(2,1)S(1)}, u32[]{:S(2)}, u32[]{:S(2)}) collective-permute-start(bf16[64]{0:T(256)(128)(2,1)S(1)} %collective-permute-done.1), channel_id=1, source_target_pairs={{3,0},{0,1},{1,2},{2,3},{7,4},{4,5},{5,6},{6,7},{11,8},{8,9},{9,10... | collective-permute-start | bytes 392 | tf_op jit(solution)/shard_map/ppermute | solution.py:12
  63.1 3.7 %collective-permute-start.4 = (bf16[64,512]{1,0:T(8,128)(2,1)S(1)}, bf16[64,512]{1,0:T(8,128)(2,1)S(1)}, u32[]{:S(2)}, u32[]{:S(2)}) collective-permute-start(bf16[64,512]{1,0:T(8,128)(2,1)S(1)} %collective-permute-done), channel_id=1, source_target_pairs={{3,0},{0,1},{1,2},{2,3},{7,4},{4,5},{5,6},{6,7},{11,8},{8,9},{9,10... | collective-permute-start | bytes 196616 | tf_op jit(solution)/shard_map/ppermute | solution.py:12
  67.0 0.7 copy-start.1
  68.5 78.3 %copy-start.2 = (f32[8]{0:T(128)S(1)}, f32[8]{0:T(128)}, u32[]{:S(2)}) copy-start(f32[8]{0:T(128)} %param.11) | copy-start | bytes 100
where the time goes:
time: 148 us; the launch traced here: 147 us
  blocking collectives  129 us (87%)
  starting transfers between devices  5.19 us (4%)
  local copies, waits for them, and re-layouts  3.66 us (2%)
  other arithmetic  3.62 us (2%)
  matrix products  3.04 us (2%)
  between operations  1.56 us (1%)
    all_gather x2, blocking collectives, merged(): everything = jax.tree.map(lambda part: lax.all_gather(part, axis), x)  74.7 us
    all_gather x1, blocking collectives, per_device(): lax.all_gather(targets, 'group', axis=0, tiled=True)  32.6 us
    unnamed x1, blocking collectives  21.3 us
    ppermute x6, starting transfers between devices, passed_along(): return lax.ppermute(block, axis, route)  5.19 us
    dot_general x4, matrix products, scores(): lax.dot_general(source_rows, target_rows, (((1,), (1,)), ((), ())), prefe...  3.04 us
  transfers between devices with their start and end apart: 6, of which 1 were waited for; matrix products, arithmetic and copies ran while one was open for 4% of the time, Pallas kernels for 0%

commit v1 on v0

--- a/solution.py
+++ b/solution.py
@@ -4,6 +4,24 @@
 from jax.sharding import PartitionSpec as P
 
 epsilon = 0.05
+
+
+def ring_gather(value, axis, dim):
+    ways, here, hop = (lax.axis_size(axis), lax.axis_index(axis), value.shape[dim])
+    lengths = [n * ways if d == dim else n for d, n in enumerate(value.shape)]
+    full = lax.dynamic_update_slice_in_dim(
+        jnp.zeros(lengths, value.dtype), value, here * hop, axis=dim
+    )
+    going_up = going_down = value
+    for far in range(1, ways // 2 + 1):
+        going_up = lax.ppermute(going_up, axis, [(d, (d + 1) % ways) for d in range(ways)])
+        full = lax.dynamic_update_slice_in_dim(full, going_up, (here - far) % ways * hop, axis=dim)
+        if 2 * far < ways:
+            going_down = lax.ppermute(going_down, axis, [(d, (d - 1) % ways) for d in range(ways)])
+            full = lax.dynamic_update_slice_in_dim(
+                full, going_down, (here + far) % ways * hop, axis=dim
+            )
+    return full
 
 
 def passed_along(block, axis, distance):
@@ -86,7 +104,7 @@
         jnp.zeros((source_count,), jnp.float32),
     )
     gathered = (
-        lax.all_gather(targets, "group", axis=0, tiled=True),
+        ring_gather(targets, "group", 0),
         lax.all_gather(target_potential, "group", axis=0, tiled=True),
     )
     own_block = lax.axis_index("blk")

time: 148 us -> 140 us (0.946)
  blocking collectives: 129 us -> 93.8 us
  starting transfers between devices: 5.19 us -> 19.3 us
  waiting for transfers between devices: 0.95 us -> 13.7 us
    all_gather x1 -> x0, blocking collectives: 32.6 us -> none  [per_device(): lax.all_gather(targets, 'group', axis=0, tiled=True)]
    ppermute x0 -> x7, starting transfers between devices: none -> 15.6 us  [the longest x3 12.5 us: ring_gather(): lax.ppermute(going_down, axis, [(d, (d - 1) % ways) for d in range(ways)])]
    ppermute x0 -> x7, waiting for transfers between devices: none -> 9.56 us  [the longest x4 9.56 us: ring_gather(): lax.ppermute(going_up, axis, [(d, (d + 1) % ways) for d in range(ways)])]
    ppermute x6, waiting for transfers between devices: 0.95 us -> 4.09 us  [passed_along(): return lax.ppermute(block, axis, route)]
    unnamed x1, blocking collectives: 21.3 us -> 19.1 us
    ppermute x6, starting transfers between devices: 5.19 us -> 3.68 us  [passed_along(): return lax.ppermute(block, axis, route)]
  transfers between devices with their start and end apart: 6 -> 13, of which waited for: 1 -> 5; matrix products, arithmetic and copies ran while one was open for 4% -> 4% of each run, Pallas kernels for 0% -> 0%
where the time goes in v1:
time: 140 us
  blocking collectives  93.8 us (67%)
  starting transfers between devices  19.3 us (14%)
  waiting for transfers between devices  13.7 us (10%)
  other arithmetic  4.84 us (3%)
  local copies, waits for them, and re-layouts  3.7 us (3%)
  matrix products  1.8 us (1%)
  between operations  1.74 us (1%)
    all_gather x2, blocking collectives, merged(): everything = jax.tree.map(lambda part: lax.all_gather(part, axis), x)  74.7 us
    unnamed x1, blocking collectives  19.1 us
    ppermute x3, starting transfers between devices, ring_gather(): lax.ppermute(going_down, axis, [(d, (d - 1) % ways) for d in range(ways)])  12.5 us
    ppermute x4, waiting for transfers between devices, ring_gather(): lax.ppermute(going_up, axis, [(d, (d + 1) % ways) for d in range(ways)])  9.56 us
    ppermute x6, waiting for transfers between devices, passed_along(): return lax.ppermute(block, axis, route)  4.09 us
    ppermute x6, starting transfers between devices, passed_along(): return lax.ppermute(block, axis, route)  3.68 us
    ppermute x4, starting transfers between devices, ring_gather(): lax.ppermute(going_up, axis, [(d, (d + 1) % ways) for d in range(ways)])  3.11 us
  transfers between devices with their start and end apart: 13, of which 5 were waited for; matrix products, arithmetic and copies ran while one was open for 4% of the time, Pallas kernels for 0%

profile of v1, /device:TPU:0, one launch (start us, length us, event | category | flops | bytes accessed | tf_op | source)
XLA Modules:
  0.0 139.6 jit_solution(5346258006883296176)
XLA Ops:
  0.6 0.0 copy-start
  0.7 3.0 %collective-permute-start = (bf16[8,512]{1,0:T(8,128)(2,1)}, bf16[8,512]{1,0:T(8,128)(2,1)S(1)}, u32[]{:S(2)}, u32[]{:S(2)}) collective-permute-start(bf16[8,512]{1,0:T(8,128)(2,1)} %param.8), channel_id=1, source_target_pairs={{0,4},{4,8},{8,12},{12,16},{16,20},{20,24},{24,28},{28,0},{1,5},{5... | collective-permute-start | bytes 24584 | tf_op jit(solution)/shard_map/ppermute | solution.py:17
  3.6 3.1 %collective-permute-start.1 = (bf16[8,512]{1,0:T(8,128)(2,1)}, bf16[8,512]{1,0:T(8,128)(2,1)S(1)}, u32[]{:S(2)}, u32[]{:S(2)}) collective-permute-start(bf16[8,512]{1,0:T(8,128)(2,1)} %param.8), channel_id=1, source_target_pairs={{0,28},{4,0},{8,4},{12,8},{16,12},{20,16},{24,20},{28,24},{1,29},{... | collective-permute-start | bytes 24584 | tf_op jit(solution)/shard_map/ppermute | solution.py:20
  6.7 1.2 dynamic-slice.8
  8.6 0.9 dynamic-update-slice
  9.5 19.1 %all-reduce = bf16[64]{0:T(256)(128)(2,1)S(1)} all-reduce(bf16[64]{0:T(256)(128)(2,1)S(1)} %dynamic-update-slice), channel_id=1, replica_groups=mesh['group'=8,'blk'=4] {'group'}, use_global_device_ids=true, to_apply=%add | all-reduce | flops 64 | bytes 256
  28.6 0.0 collective-permute-start.8
  28.6 1.7 %collective-permute-start.10 = (bf16[64]{0:T(256)(128)(2,1)S(1)}, bf16[64]{0:T(256)(128)(2,1)S(1)}, u32[]{:S(2)}, u32[]{:S(2)}) collective-permute-start(bf16[64]{0:T(256)(128)(2,1)S(1)} %all-reduce), channel_id=1, source_target_pairs={{1,0},{2,1},{3,2},{0,3},{5,4},{6,5},{7,6},{4,7},{9,8},{10,9},{11,1... | collective-permute-start | bytes 392 | tf_op jit(solution)/shard_map/ppermute | solution.py:30
  30.4 1.5 %multiply_reduce_fusion = f32[1024]{0:T(1024)S(1)} fusion(bf16[1024,512]{1,0:T(8,128)(2,1)} %param.7), kind=kLoop, calls=%fused_computation.3 | loop fusion | flops 1571840 | bytes 1052672 | tf_op jit(solution)/shard_map/reduce_sum | solution.py:143
  32.1 0.0 collective-permute-done.8
  32.1 0.1 collective-permute-start.12
  32.2 0.0 collective-permute-done
  32.2 0.1 collective-permute-start.2
  32.3 0.0 collective-permute-done.1
  32.3 4.7 %collective-permute-start.3 = (bf16[8,512]{1,0:T(8,128)(2,1)S(1)}, bf16[8,512]{1,0:T(8,128)(2,1)S(1)}, u32[]{:S(2)}, u32[]{:S(2)}) collective-permute-start(bf16[8,512]{1,0:T(8,128)(2,1)S(1)} %collective-permute-done.1), channel_id=1, source_target_pairs={{0,28},{4,0},{8,4},{12,8},{16,12},{20,16},{24,20},{28,24},{1,29},{... | collective-permute-start | bytes 24584 | tf_op jit(solution)/shard_map/ppermute | solution.py:20
  37.0 1.6 %collective-permute-done.2 = bf16[8,512]{1,0:T(8,128)(2,1)S(1)} collective-permute-done((bf16[8,512]{1,0:T(8,128)(2,1)S(1)}, bf16[8,512]{1,0:T(8,128)(2,1)S(1)}, u32[]{:S(2)}, u32[]{:S(2)}) %collective-permute-start.2) | collective-permute-done | bytes 8224 | tf_op jit(solution)/shard_map/ppermute | solution.py:17
  38.6 0.0 collective-permute-start.4
  38.6 0.0 collective-permute-done.3
  38.6 4.7 %collective-permute-start.5 = (bf16[8,512]{1,0:T(8,128)(2,1)S(1)}, bf16[8,512]{1,0:T(8,128)(2,1)S(1)}, u32[]{:S(2)}, u32[]{:S(2)}) collective-permute-start(bf16[8,512]{1,0:T(8,128)(2,1)S(1)} %collective-permute-done.3), channel_id=1, source_target_pairs={{0,28},{4,0},{8,4},{12,8},{16,12},{20,16},{24,20},{28,24},{1,29},{... | collective-permute-start | bytes 24584 | tf_op jit(solution)/shard_map/ppermute | solution.py:20
  43.3 1.6 %collective-permute-done.4 = bf16[8,512]{1,0:T(8,128)(2,1)S(1)} collective-permute-done((bf16[8,512]{1,0:T(8,128)(2,1)S(1)}, bf16[8,512]{1,0:T(8,128)(2,1)S(1)}, u32[]{:S(2)}, u32[]{:S(2)}) %collective-permute-start.4) | collective-permute-done | bytes 8224 | tf_op jit(solution)/shard_map/ppermute | solution.py:17
  44.9 0.0 collective-permute-start.6
  44.9 0.0 collective-permute-done.5
  44.9 6.3 %collective-permute-done.6 = bf16[8,512]{1,0:T(8,128)(2,1)S(1)} collective-permute-done((bf16[8,512]{1,0:T(8,128)(2,1)S(1)}, bf16[8,512]{1,0:T(8,128)(2,1)S(1)}, u32[]{:S(2)}, u32[]{:S(2)}) %collective-permute-start.6) | collective-permute-done | bytes 8224 | tf_op jit(solution)/shard_map/ppermute | solution.py:17
  51.3 0.1 multiply_reduce_fusion.4
  51.4 0.1 collective-permute-start.7
  51.4 1.7 %collective-permute-start.9 = (bf16[64,512]{1,0:T(8,128)(2,1)S(1)}, bf16[64,512]{1,0:T(8,128)(2,1)S(1)}, u32[]{:S(2)}, u32[]{:S(2)}) collective-permute-start(bf16[64,512]{1,0:T(8,128)(2,1)S(1)} %constant_dynamic-update-slice_fusion), channel_id=1, source_target_pairs={{1,0},{2,1},{3,2},{0,3},{5,4},{6,5},{7,6},{4,7},{9,8},{10,9},{11,1... | collective-permute-start | bytes 196616 | tf_op jit(solution)/shard_map/ppermute | solution.py:30
  53.2 0.4 fusion.14
  53.6 1.5 %collective-permute-done.7 = bf16[64,512]{1,0:T(8,128)(2,1)S(1)} collective-permute-done((bf16[64,512]{1,0:T(8,128)(2,1)S(1)}, bf16[64,512]{1,0:T(8,128)(2,1)S(1)}, u32[]{:S(2)}, u32[]{:S(2)}) %collective-permute-start.7) | collective-permute-done | bytes 65568 | tf_op jit(solution)/shard_map/ppermute | solution.py:30
  55.1 0.1 multiply_reduce_fusion.3
  55.2 0.1 collective-permute-start.11
  55.3 0.5 fusion.13
  55.8 0.0 collective-permute-done.9
  55.8 0.1 multiply_reduce_fusion.2
  55.9 0.0 collective-permute-done.10
  55.9 0.5 fusion.12
  56.4 2.6 %collective-permute-done.11 = bf16[64,512]{1,0:T(8,128)(2,1)S(1)} collective-permute-done((bf16[64,512]{1,0:T(8,128)(2,1)S(1)}, bf16[64,512]{1,0:T(8,128)(2,1)S(1)}, u32[]{:S(2)}, u32[]{:S(2)}) %collective-permute-start.11) | collective-permute-done | bytes 65568 | tf_op jit(solution)/shard_map/ppermute | solution.py:30
  59.0 0.1 multiply_reduce_fusion.1
  59.1 0.0 collective-permute-done.12
  59.1 0.0 copy-start.2
  59.1 0.5 fusion.11
  59.6 0.1 exponential_reduce_fusion.6
  59.7 0.1 exponential_reduce_fusion.4
  59.8 0.0 copy-done.2
  59.8 0.6 multiply_add_fusion.1
  60.4 0.2 fusion.7
  60.6 0.0 copy-start.3
  60.7 0.3 exponential_reduce_fusion
  61.0 0.3 exponential_reduce_fusion.1
  61.3 0.1 reshape_reshape.29
  61.3 0.1 reshape_reshape.28
  61.4 0.1 reshape_reshape.30
  61.5 0.1 reshape_reshape.31
  61.6 0.1 dynamic_update_slice.77
  61.8 0.1 reshape.118
  61.9 37.9 %all-gather.1 = f32[32,1,256]{2,1,0:T(1,128)S(1)} all-gather(f32[1,1,256]{2,1,0:T(1,128)S(1)} %reshape.118), channel_id=1, replica_groups=mesh['group'=8,'blk'=4] {'group','blk'}, dimensions={0}, use_global_device_ids=true | all-gather | bytes 33792 | tf_op jit(solution)/shard_map/all_gather | solution.py:34
  99.7 0.1 reshape_reshape.25
  99.8 0.1 reshape_reshape.24
  99.9 0.1 reshape_reshape.26
  100.0 0.1 reshape_reshape.27
  100.1 0.1 dynamic_update_slice.73
  100.2 0.1 reshape.116
  100.3 36.8 %all-gather = f32[32,1,256]{2,1,0:T(1,128)S(1)} all-gather(f32[1,1,256]{2,1,0:T(1,128)S(1)} %reshape.116), channel_id=1, replica_groups=mesh['group'=8,'blk'=4] {'group','blk'}, dimensions={0}, use_global_device_ids=true | all-gather | bytes 33792 | tf_op jit(solution)/shard_map/all_gather | solution.py:34
  137.2 1.8 %while.11 = (s32[]{:T(128)}, f32[256]{0:T(256)S(1)}, f32[256]{0:T(256)S(1)}, f32[32,256]{1,0:T(8,128)S(1)}, f32[32,256]{1,0:T(8,128)S(1)}, /*index=5*/s32[]{:T(128)}, s32[]{:T(128)}, s32[]{:T(128)}) while((s32[]{:T(128)}, f32[256]{0:T(256)S(1)}, f32[256]{0:T(256)S(1)}, f32[32,256]{1,0:T(8,128)S(1)}, f32[32,256]{1,0:T(8,128)S(1)}, ...), condition=%wide.region_22.23_spmd, body=%wide.region_21.22_spmd.sunk | while | flops 1541 | bytes 10371 | solution.py:40
  139.0 0.6 subtract_multiply_fusion
  (93 shorter events, 1.3 us)
Async XLA Ops:
  0.6 31.3 %copy-start.1 = (bf16[8,512]{1,0:T(8,128)(2,1)S(1)}, bf16[8,512]{1,0:T(8,128)(2,1)}, u32[]{:S(2)}) copy-start(bf16[8,512]{1,0:T(8,128)(2,1)} %param.8) | copy-start | bytes 24580
  0.6 52.6 %copy-start = (bf16[1024,512]{1,0:T(8,128)(2,1)S(1)}, bf16[1024,512]{1,0:T(8,128)(2,1)}, u32[]{:S(2)}) copy-start(bf16[1024,512]{1,0:T(8,128)(2,1)} %param.7) | copy-start | bytes 3145732
  0.7 31.5 %collective-permute-start = (bf16[8,512]{1,0:T(8,128)(2,1)}, bf16[8,512]{1,0:T(8,128)(2,1)S(1)}, u32[]{:S(2)}, u32[]{:S(2)}) collective-permute-start(bf16[8,512]{1,0:T(8,128)(2,1)} %param.8), channel_id=1, source_target_pairs={{0,4},{4,8},{8,12},{12,16},{16,20},{20,24},{24,28},{28,0},{1,5},{5... | collective-permute-start | bytes 24584 | tf_op jit(solution)/shard_map/ppermute | solution.py:17
  3.6 28.6 %collective-permute-start.1 = (bf16[8,512]{1,0:T(8,128)(2,1)}, bf16[8,512]{1,0:T(8,128)(2,1)S(1)}, u32[]{:S(2)}, u32[]{:S(2)}) collective-permute-start(bf16[8,512]{1,0:T(8,128)(2,1)} %param.8), channel_id=1, source_target_pairs={{0,28},{4,0},{8,4},{12,8},{16,12},{20,16},{24,20},{28,24},{1,29},{... | collective-permute-start | bytes 24584 | tf_op jit(solution)/shard_map/ppermute | solution.py:20
  28.6 3.5 %collective-permute-start.8 = (bf16[64]{0:T(256)(128)(2,1)S(1)}, bf16[64]{0:T(256)(128)(2,1)S(1)}, u32[]{:S(2)}, u32[]{:S(2)}) collective-permute-start(bf16[64]{0:T(256)(128)(2,1)S(1)} %all-reduce), channel_id=1, source_target_pairs={{3,0},{0,1},{1,2},{2,3},{7,4},{4,5},{5,6},{6,7},{11,8},{8,9},{9,10... | collective-permute-start | bytes 392 | tf_op jit(solution)/shard_map/ppermute | solution.py:30
  28.6 27.3 %collective-permute-start.10 = (bf16[64]{0:T(256)(128)(2,1)S(1)}, bf16[64]{0:T(256)(128)(2,1)S(1)}, u32[]{:S(2)}, u32[]{:S(2)}) collective-permute-start(bf16[64]{0:T(256)(128)(2,1)S(1)} %all-reduce), channel_id=1, source_target_pairs={{1,0},{2,1},{3,2},{0,3},{5,4},{6,5},{7,6},{4,7},{9,8},{10,9},{11,1... | collective-permute-start | bytes 392 | tf_op jit(solution)/shard_map/ppermute | solution.py:30
  32.1 27.0 %collective-permute-start.12 = (bf16[64]{0:T(256)(128)(2,1)S(1)}, bf16[64]{0:T(256)(128)(2,1)S(1)}, u32[]{:S(2)}, u32[]{:S(2)}) collective-permute-start(bf16[64]{0:T(256)(128)(2,1)S(1)} %collective-permute-done.8), channel_id=1, source_target_pairs={{3,0},{0,1},{1,2},{2,3},{7,4},{4,5},{5,6},{6,7},{11,8},{8,9},{9,10... | collective-permute-start | bytes 392 | tf_op jit(solution)/shard_map/ppermute | solution.py:30
  32.2 6.4 %collective-permute-start.2 = (bf16[8,512]{1,0:T(8,128)(2,1)S(1)}, bf16[8,512]{1,0:T(8,128)(2,1)S(1)}, u32[]{:S(2)}, u32[]{:S(2)}) collective-permute-start(bf16[8,512]{1,0:T(8,128)(2,1)S(1)} %collective-permute-done), channel_id=1, source_target_pairs={{0,4},{4,8},{8,12},{12,16},{16,20},{20,24},{24,28},{28,0},{1,5},{5... | collective-permute-start | bytes 24584 | tf_op jit(solution)/shard_map/ppermute | solution.py:17
  32.3 6.3 %collective-permute-start.3 = (bf16[8,512]{1,0:T(8,128)(2,1)S(1)}, bf16[8,512]{1,0:T(8,128)(2,1)S(1)}, u32[]{:S(2)}, u32[]{:S(2)}) collective-permute-start(bf16[8,512]{1,0:T(8,128)(2,1)S(1)} %collective-permute-done.1), channel_id=1, source_target_pairs={{0,28},{4,0},{8,4},{12,8},{16,12},{20,16},{24,20},{28,24},{1,29},{... | collective-permute-start | bytes 24584 | tf_op jit(solution)/shard_map/ppermute | solution.py:20
  38.6 6.3 %collective-permute-start.4 = (bf16[8,512]{1,0:T(8,128)(2,1)S(1)}, bf16[8,512]{1,0:T(8,128)(2,1)S(1)}, u32[]{:S(2)}, u32[]{:S(2)}) collective-permute-start(bf16[8,512]{1,0:T(8,128)(2,1)S(1)} %collective-permute-done.2), channel_id=1, source_target_pairs={{0,4},{4,8},{8,12},{12,16},{16,20},{20,24},{24,28},{28,0},{1,5},{5... | collective-permute-start | bytes 24584 | tf_op jit(solution)/shard_map/ppermute | solution.py:17
  38.6 6.3 %collective-permute-start.5 = (bf16[8,512]{1,0:T(8,128)(2,1)S(1)}, bf16[8,512]{1,0:T(8,128)(2,1)S(1)}, u32[]{:S(2)}, u32[]{:S(2)}) collective-permute-start(bf16[8,512]{1,0:T(8,128)(2,1)S(1)} %collective-permute-done.3), channel_id=1, source_target_pairs={{0,28},{4,0},{8,4},{12,8},{16,12},{20,16},{24,20},{28,24},{1,29},{... | collective-permute-start | bytes 24584 | tf_op jit(solution)/shard_map/ppermute | solution.py:20
  44.9 6.3 %collective-permute-start.6 = (bf16[8,512]{1,0:T(8,128)(2,1)S(1)}, bf16[8,512]{1,0:T(8,128)(2,1)S(1)}, u32[]{:S(2)}, u32[]{:S(2)}) collective-permute-start(bf16[8,512]{1,0:T(8,128)(2,1)S(1)} %collective-permute-done.4), channel_id=1, source_target_pairs={{0,4},{4,8},{8,12},{12,16},{16,20},{20,24},{24,28},{28,0},{1,5},{5... | collective-permute-start | bytes 24584 | tf_op jit(solution)/shard_map/ppermute | solution.py:17
  51.4 3.7 %collective-permute-start.7 = (bf16[64,512]{1,0:T(8,128)(2,1)S(1)}, bf16[64,512]{1,0:T(8,128)(2,1)S(1)}, u32[]{:S(2)}, u32[]{:S(2)}) collective-permute-start(bf16[64,512]{1,0:T(8,128)(2,1)S(1)} %constant_dynamic-update-slice_fusion), channel_id=1, source_target_pairs={{3,0},{0,1},{1,2},{2,3},{7,4},{4,5},{5,6},{6,7},{11,8},{8,9},{9,10... | collective-permute-start | bytes 196616 | tf_op jit(solution)/shard_map/ppermute | solution.py:30
  51.4 4.3 %collective-permute-start.9 = (bf16[64,512]{1,0:T(8,128)(2,1)S(1)}, bf16[64,512]{1,0:T(8,128)(2,1)S(1)}, u32[]{:S(2)}, u32[]{:S(2)}) collective-permute-start(bf16[64,512]{1,0:T(8,128)(2,1)S(1)} %constant_dynamic-update-slice_fusion), channel_id=1, source_target_pairs={{1,0},{2,1},{3,2},{0,3},{5,4},{6,5},{7,6},{4,7},{9,8},{10,9},{11,1... | collective-permute-start | bytes 196616 | tf_op jit(solution)/shard_map/ppermute | solution.py:30
  55.2 3.7 %collective-permute-start.11 = (bf16[64,512]{1,0:T(8,128)(2,1)S(1)}, bf16[64,512]{1,0:T(8,128)(2,1)S(1)}, u32[]{:S(2)}, u32[]{:S(2)}) collective-permute-start(bf16[64,512]{1,0:T(8,128)(2,1)S(1)} %collective-permute-done.7), channel_id=1, source_target_pairs={{3,0},{0,1},{1,2},{2,3},{7,4},{4,5},{5,6},{6,7},{11,8},{8,9},{9,10... | collective-permute-start | bytes 196616 | tf_op jit(solution)/shard_map/ppermute | solution.py:30
  59.1 0.7 copy-start.2
  60.6 78.3 %copy-start.3 = (f32[8]{0:T(128)S(1)}, f32[8]{0:T(128)}, u32[]{:S(2)}) copy-start(f32[8]{0:T(128)} %param.11) | copy-start | bytes 100
